TPU v7x, 512 devices: a whole 4x4x16 slice. The times are simulated.
512 devices in a mesh: tm: 64 (over z, y_hi, core), space: 8 (over y_lo, x).
Axes of the slice: x: 4, y: 4 (y_hi: 2, y_lo: 2; y = y_hi * 2 + y_lo), z: 16, core: 2. Of those that a mesh axis runs over, the one named last changes fastest.
Arguments:
- start_states: float32 [64, 256, 256], P('tm', 'space'), may hold values from -6 to 6
- region_map: int32 [256, 256], P('space'), may hold values from 0 to 3
- source: float32 [2, 256, 256], P(None, 'space'), may hold values from -6 to 6
- front: int32 [], replicated, may hold values from 33 to 63
Outputs:
- new_states: float32 [64, 256, 256], P('tm', 'space')
- jumps: float32 [64, 256, 256], P('tm', 'space')
All inputs are finite; a program needn't handle non-finite values.
Results may differ from a plain program's by a relative error of at most 0.000027.
Values sent between devices are 32-bit elements; how exact they have to be, the bound alone decides.
No kernel may reach another device: no remote copies, remote signals or barrier semaphores. Data moves between devices by JAX's collectives and lax.ppermute only.
A program may use at most 64 MiB of HBM per device.

v0:
```python
import math
import jax
import jax.numpy as jnp
from jax import lax
from jax.sharding import PartitionSpec as P

FINE = 16
ITERS = 2
RELUCTIVITY = (1.0, 0.3, 1.0, 0.25)
SATURATION = (0.0, 2.0, 0.0, 1.5)
MOBILITY = (0.15, 0.02, 0.0004, 0.0008)


def extended_2(block, sides, width):
    for axis, dim in sides:
        count = lax.axis_size(axis)
        forward = [(i, i + 1) for i in range(count - 1)]
        backward = [(target, source) for source, target in forward]
        low = lax.ppermute(
            lax.slice_in_dim(block, block.shape[dim] - width, None, axis=dim), axis, forward
        )
        high = lax.ppermute(lax.slice_in_dim(block, 0, width, axis=dim), axis, backward)
        block = jnp.concatenate([low, block, high], axis=dim)
    return block


def entering(x, axis, combine, identity):
    size, position = (lax.axis_size(axis), lax.axis_index(axis))
    everything = jax.tree.map(lambda part: lax.all_gather(part, axis), x)
    start = jax.tree.map(
        lambda part, zero: jnp.broadcast_to(jnp.asarray(zero, part.dtype), part.shape), x, identity
    )

    def hop(k, before):
        reached = k < position
        new = combine(before, jax.tree.map(lambda part: part[k], everything))
        return jax.tree.map(lambda a, b: jnp.where(reached, a, b), new, before)

    return lax.fori_loop(0, size, hop, start)


def from_root(x, axis, root):
    mine = lax.axis_index(axis) == root
    return lax.psum(jnp.where(mine, x, jnp.zeros_like(x)), axis)


def from_behind(x, axis, by):
    size = lax.axis_size(axis)
    return lax.ppermute(x, axis, [(i, (i + by) % size) for i in range(size)])


def lookup(region_map, table):
    result = jnp.zeros(region_map.shape, jnp.float32)
    for region, entry_value in enumerate(table):
        result = result + jnp.where(
            region_map == region, jnp.float32(entry_value), jnp.float32(0.0)
        )
    return result


def flux_terms(extended, reluctivity, saturation):
    field_cols = jnp.pad(extended, ((0, 0), (1, 1)))
    relu_cols = jnp.pad(reluctivity, ((0, 0), (1, 1)))
    satu_cols = jnp.pad(saturation, ((0, 0), (1, 1)))
    center = field_cols[1:-1, 1:-1]
    own_rel = relu_cols[1:-1, 1:-1]
    own_sat = satu_cols[1:-1, 1:-1]
    divergence = jnp.zeros_like(center)
    diagonal = jnp.zeros_like(center)
    for row_part, col_part in (
        (slice(0, -2), slice(1, -1)),
        (slice(2, None), slice(1, -1)),
        (slice(1, -1), slice(0, -2)),
        (slice(1, -1), slice(2, None)),
    ):
        difference = field_cols[row_part, col_part] - center
        square = difference * difference
        face_rel = 0.5 * (own_rel + relu_cols[row_part, col_part])
        face_sat = 0.5 * (own_sat + satu_cols[row_part, col_part])
        weight = face_rel * (1.0 + face_sat * square / (1.0 + square))
        divergence = divergence + weight * difference
        diagonal = diagonal + weight
    return (divergence, diagonal)


def compose_maps(earlier, later):
    return (later[0] * earlier[0], later[0] * earlier[1] + later[1])


def on_device(start_states, region_map, source, front):
    field_now = start_states[0]
    slices = lax.axis_size("tm")
    slice_index = lax.axis_index("tm")
    scale = 2.0 * math.pi / (slices * FINE)
    stacked = jnp.stack(
        [
            lookup(region_map, RELUCTIVITY),
            lookup(region_map, SATURATION),
            lookup(region_map, MOBILITY),
            source[0],
            source[1],
        ],
        0,
    )
    padded_fields = extended_2(stacked, (("space", 1),), 1)
    mobile = stacked[2]

    def advance(block, values, divergence, step_index):
        phase_angle = (slice_index * FINE + step_index).astype(jnp.float32) * scale
        current = block[3] * jnp.cos(phase_angle) + block[4] * jnp.sin(phase_angle)
        return values + block[2] * (divergence + current)

    def single_step(values, step_index):
        extended = extended_2(values, (("space", 0),), 1)
        divergence, diagonal = flux_terms(extended, padded_fields[0], padded_fields[1])
        return (advance(stacked, values, divergence, step_index), diagonal)

    cut_slice = (front - 1) % slices
    keep_map = slice_index != cut_slice
    fine_end = field_now
    for sweep in range(ITERS):
        fine_values = field_now
        fine_values, fine_diagonal = single_step(fine_values, 0)

        def single_turn(counter, current_values):
            return single_step(current_values, counter)[0]

        fine_values = lax.fori_loop(1, FINE, single_turn, fine_values)
        fine_end = fine_values
        diagonal = fine_diagonal
        decay = 1.0 / (1.0 + FINE * mobile * diagonal)
        decay = jnp.where(keep_map, decay, 0.0)
        offset = fine_end - decay * field_now
        prefix = entering(
            (decay, offset), "tm", compose_maps, (jnp.ones_like(decay), jnp.zeros_like(offset))
        )
        total = compose_maps(prefix, (decay, offset))
        closing = from_root(total[1], "tm", slices - 1)
        field_now = prefix[0] * closing + prefix[1]
    jumps = from_behind(fine_end, "tm", 1) - field_now
    return (field_now[None], jumps[None])


def solution(mesh):
    placed = (P("tm", "space", None), P("space", None), P(None, "space", None), P())
    return jax.shard_map(
        on_device,
        mesh=mesh,
        in_specs=placed,
        out_specs=(P("tm", "space", None), P("tm", "space", None)),
        check_vma=False,
    )
```

profile of v0, /device:TPU:2, one launch (start us, length us, event | category | flops | bytes accessed | tf_op | source)
XLA Modules:
  0.0 1535.7 jit_solution(15619786963016849872)
XLA Ops:
  29.0 142.5 %while.62 = (s32[]{:T(128)}, f32[32,256]{1,0:T(8,128)S(1)}, f32[32,256]{1,0:T(8,128)S(1)}, f32[32,256]{1,0:T(8,128)S(1)}, f32[32,256]{1,0:T(8,128)S(1)}, /*index...) while((s32[]{:T(128)}, f32[32,256]{1,0:T(8,128)S(1)}, ...), condition=%wide.region_1.2_spmd, body=%wide.region_0.1_spmd.sunk | while | flops 520741 | bytes 784917 | solution.py:128
  56.2 6.3 collective-permute-start.1
  66.0 6.3 collective-permute-start.1
  75.7 6.3 collective-permute-start.1
  85.5 6.3 collective-permute-start.1
  95.3 6.3 collective-permute-start.1
  105.0 6.3 collective-permute-start.1
  124.6 6.3 collective-permute-start.1
  134.3 6.3 collective-permute-start.1
  144.1 6.3 collective-permute-start.1
  153.8 6.3 collective-permute-start.1
  173.0 153.9 %all-gather.9.cloned.1.call-done = f32[2048,256]{1,0:T(8,128)} async-done(((f32[32,256]{1,0:T(8,128)}), f32[2048,256]{1,0:T(8,128)}) %all-gather.9.cloned.1.call-update) | async-done | bytes 2097168 | tf_op jit(solution)/shard_map/all_gather | solution.py:29
  326.9 142.1 %all-gather.11.cloned.1.call-done = f32[2048,256]{1,0:T(8,128)} async-done(((f32[32,256]{1,0:T(8,128)}), f32[2048,256]{1,0:T(8,128)}) %all-gather.11.cloned.1.call-update) | async-done | bytes 2097168 | tf_op jit(solution)/shard_map/all_gather | solution.py:29
  469.0 52.4 %while.64 = (s32[]{:T(128)}, f32[32,256]{1,0:T(8,128)S(1)}, f32[32,256]{1,0:T(8,128)S(1)}, s32[]{:T(128)}, f32[64,32,256]{2,1,0:T(8,128)}, /*index=5*/f32[64,32,256]{2,1,0:T(8,128)}, s32[]{:T(128)}, s32[]{:T(128)}) while((s32[]{:T(128)}, f32[32,256]{1,0:T(8,128)S(1)}, f32[32,256]{1,0:T(8,128)S(1)}, s32[]{:T(128)}, ...), condition=%wide.region_3.4_spmd.clone, body=%wide.region_2.3_spmd.clone.sunk | while | flops 57348 | bytes 196717 | solution.py:39
  522.2 257.2 %psum.14 = f32[32,256]{1,0:T(8,128)S(1)} all-reduce(f32[32,256]{1,0:T(8,128)S(1)} %add_select_fusion.1), channel_id=1, replica_groups=mesh['tm'=64,'space'=8] {'tm'}, use_global_device_ids=true, to_apply=%region_4.5 | all-reduce | flops 8192 | bytes 65536 | tf_op jit(solution)/shard_map/psum | solution.py:44
  788.4 142.2 %while.63 = (s32[]{:T(128)}, f32[32,256]{1,0:T(8,128)S(1)}, f32[32,256]{1,0:T(8,128)S(1)}, f32[32,256]{1,0:T(8,128)S(1)}, f32[32,256]{1,0:T(8,128)S(1)}, /*index...) while((s32[]{:T(128)}, f32[32,256]{1,0:T(8,128)S(1)}, ...), condition=%wide.region_6.7_spmd, body=%wide.region_5.6_spmd.sunk | while | flops 520741 | bytes 784917 | solution.py:128
  854.5 6.3 collective-permute-start.3
  864.3 6.3 collective-permute-start.3
  874.0 6.3 collective-permute-start.3
  883.8 6.3 collective-permute-start.3
  933.9 142.4 %all-gather.13.cloned.1.call-done = f32[2048,256]{1,0:T(8,128)} async-done(((f32[32,256]{1,0:T(8,128)}), f32[2048,256]{1,0:T(8,128)}) %all-gather.13.cloned.1.call-update) | async-done | bytes 2097168 | tf_op jit(solution)/shard_map/all_gather | solution.py:29
  1076.3 141.9 %all-gather.15.cloned.1.call-done = f32[2048,256]{1,0:T(8,128)} async-done(((f32[32,256]{1,0:T(8,128)}), f32[2048,256]{1,0:T(8,128)}) %all-gather.15.cloned.1.call-update) | async-done | bytes 2097168 | tf_op jit(solution)/shard_map/all_gather | solution.py:29
  1218.2 52.4 %while.65 = (s32[]{:T(128)}, f32[32,256]{1,0:T(8,128)S(1)}, f32[32,256]{1,0:T(8,128)S(1)}, s32[]{:T(128)}, f32[64,32,256]{2,1,0:T(8,128)}, /*index=5*/f32[64,32,256]{2,1,0:T(8,128)}, s32[]{:T(128)}, s32[]{:T(128)}) while((s32[]{:T(128)}, f32[32,256]{1,0:T(8,128)S(1)}, f32[32,256]{1,0:T(8,128)S(1)}, s32[]{:T(128)}, ...), condition=%wide.region_8.9_spmd.clone, body=%wide.region_7.8_spmd.clone.sunk | while | flops 57348 | bytes 196717 | solution.py:39
  1271.4 257.2 %psum.15 = f32[32,256]{1,0:T(8,128)S(1)} all-reduce(f32[32,256]{1,0:T(8,128)S(1)} %add_select_fusion), channel_id=1, replica_groups=mesh['tm'=64,'space'=8] {'tm'}, use_global_device_ids=true, to_apply=%region_9.10 | all-reduce | flops 8192 | bytes 65536 | tf_op jit(solution)/shard_map/psum | solution.py:44
  (432 shorter events, 328.2 us)
Async XLA Ops:
  7.2 319.8 %all-gather.9.cloned.1.call-start = ((), (), s32[]{:S(2)}) async-start(), calls=%async_computation | async-start | bytes 2129920 | tf_op jit(solution)/shard_map/all_gather | solution.py:29
  8.8 18.2 %collective-permute-start.4 = (f32[5,1,256]{2,1,0:T(1,128)S(1)}, f32[5,1,256]{2,1,0:T(1,128)S(1)}, u32[]{:S(2)}, u32[]{:S(2)}) collective-permute-start(f32[5,1,256]{2,1,0:T(1,128)S(1)} %get-tuple-element.769), channel_id=1, source_target_pairs={{0,1},{1,2},{2,3},{3,4},{4,5},{5,6},{6,7},{8,9},{9,10},{10,11},{11... | collective-permute-start | bytes 15368 | tf_op jit(solution)/shard_map/ppermute | solution.py:19
  12.2 14.8 collective-permute-start.6
  54.3 8.4 collective-permute-start
  64.1 8.4 collective-permute-start
  73.8 8.4 collective-permute-start
  83.6 8.4 collective-permute-start
  93.3 8.4 collective-permute-start
  122.6 8.4 collective-permute-start
  132.4 8.4 collective-permute-start
  142.2 8.4 collective-permute-start
  151.9 8.4 collective-permute-start
  161.7 8.4 collective-permute-start
  172.2 296.8 %all-gather.11.cloned.1.call-start = ((), (), s32[]{:S(2)}) async-start(), calls=%async_computation.1 | async-start | bytes 2129920 | tf_op jit(solution)/shard_map/all_gather | solution.py:29
  172.9 903.4 %all-gather.13.cloned.1.call-start = ((), (), s32[]{:S(2)}) async-start(), calls=%async_computation.2 | async-start | bytes 2129920 | tf_op jit(solution)/shard_map/all_gather | solution.py:29
  813.5 8.4 collective-permute-start.2
  823.3 8.4 collective-permute-start.2
  842.8 8.4 collective-permute-start.2
  852.6 8.4 collective-permute-start.2
  862.3 8.4 collective-permute-start.2
  872.1 8.4 collective-permute-start.2
  881.9 8.4 collective-permute-start.2
  931.4 286.9 %all-gather.15.cloned.1.call-start = ((), (), s32[]{:S(2)}) async-start(), calls=%async_computation.3 | async-start | bytes 2129920 | tf_op jit(solution)/shard_map/all_gather | solution.py:29
  932.0 596.6 %collective-permute-start.10 = (f32[32,256]{1,0:T(8,128)S(1)}, f32[32,256]{1,0:T(8,128)S(1)}, u32[]{:S(2)}, u32[]{:S(2)}) collective-permute-start(f32[32,256]{1,0:T(8,128)S(1)} %get-tuple-element.623), channel_id=1, source_target_pairs={{0,8},{8,16},{16,24},{24,32},{32,40},{40,48},{48,56},{56,64},{64,7... | collective-permute-start | bytes 98312 | tf_op jit(solution)/shard_map/ppermute | solution.py:49
  (49 other events, 1097.7 us)
Sparse Core Ops, SparseCore 0:
  172.3 154.6 all-gather.8
  330.8 138.1 all-gather.10
  931.5 144.7 all-gather.12
  1080.0 138.1 all-gather.14
where the time goes:
time: 1550 us; the launch traced here: 1540 us
  waiting for transfers between devices  621 us (40%)
  blocking collectives  514 us (33%)
  starting transfers between devices  257 us (17%)
  other arithmetic  116 us (7%)
    all_gather x4, waiting for transfers between devices, entering(): everything = jax.tree.map(lambda part: lax.all_gather(part, axis), x)  580 us
    psum x2, blocking collectives, from_root(): return lax.psum(jnp.where(mine, x, jnp.zeros_like(x)), axis)  514 us
    ppermute x33, starting transfers between devices, extended_2(): lax.ppermute(lax.slice_in_dim(block, block.shape[dim] - width, None, axis...  183 us
    select_n x128, other arithmetic, hop(): return jax.tree.map(lambda a, b: jnp.where(reached, a, b), new, before)  102 us
    ppermute x33, starting transfers between devices, extended_2(): lax.ppermute(lax.slice_in_dim(block, 0, width, axis=dim), axis, backward)  72.1 us
    ppermute x33, waiting for transfers between devices, extended_2(): lax.ppermute(lax.slice_in_dim(block, block.shape[dim] - width, None, axis...  36.1 us
  transfers between devices with their start and end apart: 71, of which 35 were waited for; matrix products, arithmetic and copies ran while one was open for 4% of the time, Pallas kernels for 0%

commit v1 on v0

--- a/solution.py
+++ b/solution.py
@@ -41,7 +41,7 @@
 
 def from_root(x, axis, root):
     mine = lax.axis_index(axis) == root
-    return lax.psum(jnp.where(mine, x, jnp.zeros_like(x)), axis)
+    return jnp.sum(lax.all_gather(jnp.where(mine, x, jnp.zeros_like(x)), axis), axis=0)
 
 
 def from_behind(x, axis, by):

time: 1550 us -> 1320 us (0.85)
  the two profiles are of different devices: /device:TPU:2 before, /device:TPU:1 now
where the time goes in v1:
time: 1320 us; the launch traced here: 1300 us
  waiting for transfers between devices  921 us (70%)
  starting transfers between devices  235 us (18%)
  other arithmetic  121 us (9%)
  between operations  15.2 us (1%)
    all_gather x4, waiting for transfers between devices, entering(): everything = jax.tree.map(lambda part: lax.all_gather(part, axis), x)  625 us
    all_gather x2, waiting for transfers between devices, from_root(): lax.all_gather(jnp.where(mine, x, jnp.zeros_like(x)), axis)  274 us
    ppermute x33, starting transfers between devices, extended_2(): lax.ppermute(lax.slice_in_dim(block, block.shape[dim] - width, None, axis...  190 us
    select_n x128, other arithmetic, hop(): return jax.tree.map(lambda a, b: jnp.where(reached, a, b), new, before)  102 us
    ppermute x33, starting transfers between devices, extended_2(): lax.ppermute(lax.slice_in_dim(block, 0, width, axis=dim), axis, backward)  42.6 us
  transfers between devices with their start and end apart: 73, of which 38 were waited for; matrix products, arithmetic and copies ran while one was open for 0% of the time, Pallas kernels for 0%

profile of v1, /device:TPU:1, one launch (start us, length us, event | category | flops | bytes accessed | tf_op | source)
XLA Modules:
  0.0 1304.4 jit_solution(5232958034543665809)
XLA Ops:
  25.9 125.1 %while.62 = (s32[]{:T(128)}, f32[32,256]{1,0:T(8,128)S(1)}, f32[32,256]{1,0:T(8,128)S(1)}, f32[32,256]{1,0:T(8,128)S(1)}, f32[32,256]{1,0:T(8,128)S(1)}, /*index...) while((s32[]{:T(128)}, f32[32,256]{1,0:T(8,128)S(1)}, ...), condition=%wide.region_1.2_spmd, body=%wide.region_0.1_spmd.sunk | while | flops 520741 | bytes 784917 | solution.py:128
  57.6 6.3 collective-permute-start.1
  66.2 6.3 collective-permute-start.1
  74.8 6.3 collective-permute-start.1
  83.4 6.3 collective-permute-start.1
  92.1 6.3 collective-permute-start.1
  100.7 6.3 collective-permute-start.1
  135.1 6.3 collective-permute-start.1
  143.8 6.3 collective-permute-start.1
  152.6 175.6 %all-gather.13.cloned.1.call-done = f32[2048,256]{1,0:T(8,128)} async-done(((f32[32,256]{1,0:T(8,128)}), f32[2048,256]{1,0:T(8,128)}) %all-gather.13.cloned.1.call-update) | async-done | bytes 2097168 | tf_op jit(solution)/shard_map/all_gather | solution.py:29
  328.2 142.1 %all-gather.15.cloned.1.call-done = f32[2048,256]{1,0:T(8,128)} async-done(((f32[32,256]{1,0:T(8,128)}), f32[2048,256]{1,0:T(8,128)}) %all-gather.15.cloned.1.call-update) | async-done | bytes 2097168 | tf_op jit(solution)/shard_map/all_gather | solution.py:29
  470.3 52.4 %while.64 = (s32[]{:T(128)}, f32[32,256]{1,0:T(8,128)S(1)}, f32[32,256]{1,0:T(8,128)S(1)}, s32[]{:T(128)}, f32[64,32,256]{2,1,0:T(8,128)}, /*index=5*/f32[64,32,256]{2,1,0:T(8,128)}, s32[]{:T(128)}, s32[]{:T(128)}) while((s32[]{:T(128)}, f32[32,256]{1,0:T(8,128)S(1)}, f32[32,256]{1,0:T(8,128)S(1)}, s32[]{:T(128)}, ...), condition=%wide.region_3.4_spmd.clone, body=%wide.region_2.3_spmd.clone.sunk | while | flops 57348 | bytes 196717 | solution.py:39
  524.1 138.3 %all-gather.17.cloned.1.call-done = f32[2048,256]{1,0:T(8,128)} async-done(((f32[32,256]{1,0:T(8,128)}), f32[2048,256]{1,0:T(8,128)}) %all-gather.17.cloned.1.call-update) | async-done | bytes 2097168 | tf_op jit(solution)/shard_map/all_gather | solution.py:44
  671.8 122.0 %while.63 = (s32[]{:T(128)}, f32[32,256]{1,0:T(8,128)S(1)}, f32[32,256]{1,0:T(8,128)S(1)}, f32[32,256]{1,0:T(8,128)S(1)}, f32[32,256]{1,0:T(8,128)S(1)}, /*index...) while((s32[]{:T(128)}, f32[32,256]{1,0:T(8,128)S(1)}, ...), condition=%wide.region_6.7_spmd, body=%wide.region_5.6_spmd.sunk | while | flops 520741 | bytes 784917 | solution.py:128
  700.4 6.3 collective-permute-start.3
  734.9 6.3 collective-permute-start.3
  743.5 6.3 collective-permute-start.3
  769.4 6.3 collective-permute-start.3
  778.0 6.3 collective-permute-start.3
  786.6 6.3 collective-permute-start.3
  795.3 165.9 %all-gather.19.cloned.1.call-done = f32[2048,256]{1,0:T(8,128)} async-done(((f32[32,256]{1,0:T(8,128)}), f32[2048,256]{1,0:T(8,128)}) %all-gather.19.cloned.1.call-update) | async-done | bytes 2097168 | tf_op jit(solution)/shard_map/all_gather | solution.py:29
  961.1 141.9 %all-gather.21.cloned.1.call-done = f32[2048,256]{1,0:T(8,128)} async-done(((f32[32,256]{1,0:T(8,128)}), f32[2048,256]{1,0:T(8,128)}) %all-gather.21.cloned.1.call-update) | async-done | bytes 2097168 | tf_op jit(solution)/shard_map/all_gather | solution.py:29
  1103.0 52.4 %while.65 = (s32[]{:T(128)}, f32[32,256]{1,0:T(8,128)S(1)}, f32[32,256]{1,0:T(8,128)S(1)}, s32[]{:T(128)}, f32[64,32,256]{2,1,0:T(8,128)}, /*index=5*/f32[64,32,256]{2,1,0:T(8,128)}, s32[]{:T(128)}, s32[]{:T(128)}) while((s32[]{:T(128)}, f32[32,256]{1,0:T(8,128)S(1)}, f32[32,256]{1,0:T(8,128)S(1)}, s32[]{:T(128)}, ...), condition=%wide.region_8.9_spmd.clone, body=%wide.region_7.8_spmd.clone.sunk | while | flops 57348 | bytes 196717 | solution.py:39
  1159.1 136.0 %all-gather.23.cloned.1.call-done = f32[2048,256]{1,0:T(8,128)} async-done(((f32[32,256]{1,0:T(8,128)}), f32[2048,256]{1,0:T(8,128)}) %all-gather.23.cloned.1.call-update) | async-done | bytes 2097168 | tf_op jit(solution)/shard_map/all_gather | solution.py:44
  (438 shorter events, 290.8 us)
Async XLA Ops:
  7.2 321.0 %all-gather.13.cloned.1.call-start = ((), (), s32[]{:S(2)}) async-start(), calls=%async_computation | async-start | bytes 2129920 | tf_op jit(solution)/shard_map/all_gather | solution.py:29
  8.8 15.1 %collective-permute-start.4 = (f32[5,1,256]{2,1,0:T(1,128)S(1)}, f32[5,1,256]{2,1,0:T(1,128)S(1)}, u32[]{:S(2)}, u32[]{:S(2)}) collective-permute-start(f32[5,1,256]{2,1,0:T(1,128)S(1)} %get-tuple-element.769), channel_id=1, source_target_pairs={{0,1},{1,2},{2,3},{3,4},{4,5},{5,6},{6,7},{8,9},{9,10},{10,11},{11... | collective-permute-start | bytes 15368 | tf_op jit(solution)/shard_map/ppermute | solution.py:19
  12.7 11.2 collective-permute-start.6
  56.3 7.8 collective-permute-start
  64.9 7.8 collective-permute-start
  73.5 7.8 collective-permute-start
  82.1 7.8 collective-permute-start
  99.4 7.8 collective-permute-start
  116.6 7.8 collective-permute-start
  125.2 7.8 collective-permute-start
  133.8 7.8 collective-permute-start
  142.5 7.8 collective-permute-start
  151.8 318.5 %all-gather.15.cloned.1.call-start = ((), (), s32[]{:S(2)}) async-start(), calls=%async_computation.1 | async-start | bytes 2129920 | tf_op jit(solution)/shard_map/all_gather | solution.py:29
  152.5 509.9 %all-gather.17.cloned.1.call-start = ((), (), s32[]{:S(2)}) async-start(), calls=%async_computation.2 | async-start | bytes 2129920 | tf_op jit(solution)/shard_map/all_gather | solution.py:44
  524.1 437.1 %all-gather.19.cloned.1.call-start = ((), (), s32[]{:S(2)}) async-start(), calls=%async_computation.3 | async-start | bytes 2129920 | tf_op jit(solution)/shard_map/all_gather | solution.py:29
  699.1 7.8 collective-permute-start.2
  716.4 7.8 collective-permute-start.2
  725.0 7.8 collective-permute-start.2
  733.6 7.8 collective-permute-start.2
  742.2 7.8 collective-permute-start.2
  759.4 7.8 collective-permute-start.2
  794.6 308.4 %all-gather.21.cloned.1.call-start = ((), (), s32[]{:S(2)}) async-start(), calls=%async_computation.4 | async-start | bytes 2129920 | tf_op jit(solution)/shard_map/all_gather | solution.py:29
  795.2 500.0 %all-gather.23.cloned.1.call-start = ((), (), s32[]{:S(2)}) async-start(), calls=%async_computation.5 | async-start | bytes 2129920 | tf_op jit(solution)/shard_map/all_gather | solution.py:44
  1156.8 140.1 %collective-permute-start.10 = (f32[32,256]{1,0:T(8,128)S(1)}, f32[32,256]{1,0:T(8,128)S(1)}, u32[]{:S(2)}, u32[]{:S(2)}) collective-permute-start(f32[32,256]{1,0:T(8,128)S(1)} %get-tuple-element.623), channel_id=1, source_target_pairs={{0,8},{8,16},{16,24},{24,32},{32,40},{40,48},{48,56},{56,64},{64,7... | collective-permute-start | bytes 98312 | tf_op jit(solution)/shard_map/ppermute | solution.py:49
  (51 other events, 972.2 us)
Sparse Core Ops, SparseCore 0:
  151.9 176.2 all-gather.12
  332.1 138.1 all-gather.14
  524.2 138.1 all-gather.16
  794.7 166.3 all-gather.18
  964.8 138.1 all-gather.20
  1157.0 138.1 all-gather.22
